TPU v7x, 32 devices: a whole 2x2x4 slice. The times are simulated.
32 devices in a mesh: ri: 4 (over z), ao: 8 (over y, x, core).
Axes of the slice: x: 2, y: 2, z: 4, core: 2. Of those that a mesh axis runs over, the one named last changes fastest.
Arguments:
- tensor: bfloat16 [512, 256, 256], P('ri', 'ao'), may hold values from -0.5 to 0.5
- live_blocks: int32 [8, 8, 8], P('ri', 'ao'), may hold values 0 or 1
- occ_density: bfloat16 [256, 256], P('ao'), may hold values from -0.375 to 0.375
- virt_density: bfloat16 [256, 256], P('ao'), may hold values from -0.375 to 0.375
- occ_mask: int32 [8, 8], P('ao'), may hold values 0 or 1
- virt_mask: int32 [8, 8], P('ao'), may hold values 0 or 1
- pair_slots: int32 [8, 8], P('ao'), may hold values from 0 to 7, as said below
Outputs:
- polar: float32 [512, 512], P('ri', 'ao')
Inputs may be any that keep to these rules, and one draw needn't show every extreme that they name: pair_slots[b, 0] = b, and the 8 entries of a row are different AO blocks.
All inputs are finite; a program needn't handle non-finite values. No bound on the sum of `live_blocks` or of `occ_mask` or of `virt_mask` on one device may be relied on, other than what follows from the above.
Results may differ from a plain program's by a relative error of at most 0.0041.
Values may be sent and summed in bfloat16 or wider, within the bound.
No kernel may reach another device: no remote copies, remote signals or barrier semaphores. Data moves between devices by JAX's collectives and lax.ppermute only.
A program may use at most 192 MiB of HBM per device.

v0:
```python
import jax
import jax.numpy as jnp
from jax import lax
from jax.sharding import PartitionSpec as P

BS = 32
KS = 8
RB = 64


def shifted(block, axis, distance):
    devices = range(lax.axis_size(axis))
    route = [((i - distance) % len(devices), i) for i in devices]
    return lax.ppermute(block, axis, route)


def screen_density(density, block_mask):
    own_blocks = block_mask.shape[0]
    all_blocks = block_mask.shape[1]
    shaped = density.reshape(own_blocks, BS, all_blocks, BS)
    keeper = block_mask.astype(density.dtype)[:, None, :, None]
    return (shaped * keeper).reshape(density.shape)


def pick_slots(pair_slots, stacked, first_block):
    own_blocks = stacked.shape[1] // BS
    block_ids = first_block + jnp.arange(own_blocks, dtype=jnp.int32)
    matches = (pair_slots[:, :, None] == block_ids[None, None, :]).astype(jnp.bfloat16)
    shaped = stacked.reshape(2, own_blocks, BS, stacked.shape[2])
    return jnp.einsum("bkc,tcjn->tbkjn", matches, shaped, preferred_element_type=jnp.float32)


def per_device(tensor, live_blocks, occ_density, virt_density, occ_mask, virt_mask, pair_slots):
    own_rows = tensor.shape[0]
    own_width = tensor.shape[1]
    own_blocks = own_width // BS
    groups = live_blocks.shape[0]
    keeper = live_blocks.astype(jnp.bfloat16)[:, None, :, None, :, None]
    tensor_eff = (tensor.reshape(groups, RB, own_blocks, BS, KS, BS) * keeper).reshape(tensor.shape)
    stacked = jnp.stack(
        [screen_density(occ_density, occ_mask), screen_density(virt_density, virt_mask)]
    )
    ao_total = stacked.shape[2]
    cycle_size = lax.axis_size("ao")
    position = lax.axis_index("ao")

    def visit(turn_index, state):
        current, gathered_rows = state
        current = shifted(current, "ao", 1)
        source = (position - turn_index + cycle_size) % cycle_size
        return (current, gathered_rows + pick_slots(pair_slots, current, source * own_blocks))

    start_pick = pick_slots(pair_slots, stacked, position * own_blocks)
    unused, picked = lax.fori_loop(1, cycle_size, visit, (stacked, start_pick))
    picked = picked.astype(jnp.bfloat16)
    occ_rows = picked[0]
    virt_rows = picked[1]
    span_cols = min(128, ao_total)
    piece_count = ao_total // span_cols
    tensor_five = tensor_eff.reshape(own_rows, own_blocks, BS, KS, BS)
    occ_pieces = occ_rows.reshape(own_blocks, KS, BS, piece_count, span_cols)

    def occ_piece(piece_index):
        columns = lax.dynamic_index_in_dim(occ_pieces, piece_index, 3, keepdims=False)
        product = jnp.einsum(
            "pbikj,bkjl->lbip", tensor_five, columns, preferred_element_type=jnp.float32
        )
        return product.astype(jnp.bfloat16).reshape(span_cols, own_width, own_rows)

    half_occ = lax.map(occ_piece, jnp.arange(piece_count, dtype=jnp.int32)).reshape(
        ao_total, own_width, own_rows
    )
    half_occ_local = lax.all_to_all(half_occ, "ao", split_axis=0, concat_axis=1, tiled=True)

    def virt_piece(source_rows, piece_index):
        columns = lax.dynamic_slice_in_dim(virt_rows, piece_index * span_cols, span_cols, 3)
        product = jnp.einsum(
            "qbikj,bkjn->qbin", source_rows, columns, preferred_element_type=jnp.float32
        )
        return product.astype(jnp.bfloat16).reshape(source_rows.shape[0], own_width, span_cols)

    all_tensor = lax.all_gather(tensor_eff, "ri", axis=0, tiled=True)
    kept_rows = all_tensor.shape[0] // cycle_size
    source_rows = all_tensor
    polar_source_rows = source_rows.reshape(kept_rows * lax.axis_size("ao"), own_blocks, BS, KS, BS)

    def add_piece(piece_index, running):
        virt_part = virt_piece(polar_source_rows, piece_index)
        occ_part = lax.dynamic_slice_in_dim(half_occ_local, piece_index * span_cols, span_cols, 1)
        return running + jnp.einsum(
            "qln,lnp->qp", virt_part, occ_part, preferred_element_type=jnp.float32
        )

    polar_block = lax.psum_scatter(
        lax.fori_loop(
            0,
            piece_count,
            add_piece,
            jnp.zeros((polar_source_rows.shape[0], own_rows), jnp.float32),
        ),
        "ao",
        scatter_dimension=0,
        tiled=True,
    )
    return polar_block.T


def solution(mesh):
    placed = (
        P("ri", "ao", None),
        P("ri", "ao", None),
        P("ao", None),
        P("ao", None),
        P("ao", None),
        P("ao", None),
        P("ao", None),
    )
    return jax.shard_map(
        per_device, mesh=mesh, in_specs=placed, out_specs=P("ri", "ao"), check_vma=False
    )
```

profile of v0, /device:TPU:0, one launch (start us, length us, event | category | flops | bytes accessed | tf_op | source)
XLA Modules:
  0.0 228.5 jit_solution(457382478721264577)
XLA Ops:
  6.5 0.7 convert_element_type.41
  7.2 0.1 copy.51
  7.3 0.1 mul.93
  7.5 0.1 mul.94
  7.6 0.1 copy.41
  7.7 3.1 %broadcast_multiply_fusion.1 = bf16[128,32,256]{2,1,0:T(8,128)(2,1)} fusion(bf16[128,32,256]{2,1,0:T(8,128)(2,1)} %param.13, bf16[128,256]{1,0:T(8,128)(2,1)S(1)} %copy.41), kind=kLoop, calls=%fused_computation.23 | loop fusion | flops 1048576 | bytes 4259840 | tf_op jit(solution)/shard_map/mul | solution.py:39
  10.9 1.6 copy-done.1
  12.5 3.1 %copy.43 = bf16[128,32,256]{0,2,1:T(8,128)(2,1)} copy(bf16[128,32,256]{2,1,0:T(8,128)(2,1)S(1)} %copy-done.1) | data formatting | bytes 4194304 | tf_op args[0]
  16.0 0.1 multiply_bitcast_fusion
  16.1 32.0 %while.41 = (s32[]{:T(128)}, bf16[2,32,256]{2,1,0:T(8,128)(2,1)S(1)}, f32[2,1,8,32,256]{4,3,2,1,0:T(8,128)S(1)}, s32[]{:T(128)}, s32[1,8]{1,0:T(1,128)S(1)}, /*index=5*/s32[]{:T(128)}, s32[]{:T(128)}, s32[]{:T(128)}, s32[]{:T(128)}) while((s32[]{:T(128)}, bf16[2,32,256]{2,1,0:T(8,128)(2,1)S(1)}, f32[2,1,8,32,256]{4,3,2,1,0:T(8,128)S(1)}, ...), condition=%wide.region_1.2_spmd, body=%wide.region_0.1_spmd.sunk | while | flops 278559 | bytes 1409390 | solution.py:54
  16.1 0.5 collective-permute-start
  16.6 4.5 %collective-permute-done = bf16[2,32,256]{2,1,0:T(8,128)(2,1)S(1)} collective-permute-done((bf16[2,32,256]{2,1,0:T(8,128)(2,1)S(1)}, bf16[2,32,256]{2,1,0:T(8,128)(2,1)S(1)}, u32[]{:S(2)}, u32[]{:S(2)}) %collective-permute-start) | collective-permute-done | bytes 32800 | tf_op jit(solution)/shard_map/while/body/eval_jaxpr/ppermute | solution.py:14
  21.1 0.1 bitcast_add_fusion.2
  21.3 4.2 %collective-permute-done = bf16[2,32,256]{2,1,0:T(8,128)(2,1)S(1)} collective-permute-done((bf16[2,32,256]{2,1,0:T(8,128)(2,1)S(1)}, bf16[2,32,256]{2,1,0:T(8,128)(2,1)S(1)}, u32[]{:S(2)}, u32[]{:S(2)}) %collective-permute-start) | collective-permute-done | bytes 32800 | tf_op jit(solution)/shard_map/while/body/eval_jaxpr/ppermute | solution.py:14
  25.5 0.1 bitcast_add_fusion.2
  25.8 4.2 %collective-permute-done = bf16[2,32,256]{2,1,0:T(8,128)(2,1)S(1)} collective-permute-done((bf16[2,32,256]{2,1,0:T(8,128)(2,1)S(1)}, bf16[2,32,256]{2,1,0:T(8,128)(2,1)S(1)}, u32[]{:S(2)}, u32[]{:S(2)}) %collective-permute-start) | collective-permute-done | bytes 32800 | tf_op jit(solution)/shard_map/while/body/eval_jaxpr/ppermute | solution.py:14
  30.0 0.1 bitcast_add_fusion.2
  30.3 4.2 %collective-permute-done = bf16[2,32,256]{2,1,0:T(8,128)(2,1)S(1)} collective-permute-done((bf16[2,32,256]{2,1,0:T(8,128)(2,1)S(1)}, bf16[2,32,256]{2,1,0:T(8,128)(2,1)S(1)}, u32[]{:S(2)}, u32[]{:S(2)}) %collective-permute-start) | collective-permute-done | bytes 32800 | tf_op jit(solution)/shard_map/while/body/eval_jaxpr/ppermute | solution.py:14
  34.5 0.1 bitcast_add_fusion.2
  34.8 4.2 %collective-permute-done = bf16[2,32,256]{2,1,0:T(8,128)(2,1)S(1)} collective-permute-done((bf16[2,32,256]{2,1,0:T(8,128)(2,1)S(1)}, bf16[2,32,256]{2,1,0:T(8,128)(2,1)S(1)}, u32[]{:S(2)}, u32[]{:S(2)}) %collective-permute-start) | collective-permute-done | bytes 32800 | tf_op jit(solution)/shard_map/while/body/eval_jaxpr/ppermute | solution.py:14
  39.0 0.1 bitcast_add_fusion.2
  39.2 4.2 %collective-permute-done = bf16[2,32,256]{2,1,0:T(8,128)(2,1)S(1)} collective-permute-done((bf16[2,32,256]{2,1,0:T(8,128)(2,1)S(1)}, bf16[2,32,256]{2,1,0:T(8,128)(2,1)S(1)}, u32[]{:S(2)}, u32[]{:S(2)}) %collective-permute-start) | collective-permute-done | bytes 32800 | tf_op jit(solution)/shard_map/while/body/eval_jaxpr/ppermute | solution.py:14
  43.4 0.1 bitcast_add_fusion.2
  43.7 4.2 %collective-permute-done = bf16[2,32,256]{2,1,0:T(8,128)(2,1)S(1)} collective-permute-done((bf16[2,32,256]{2,1,0:T(8,128)(2,1)S(1)}, bf16[2,32,256]{2,1,0:T(8,128)(2,1)S(1)}, u32[]{:S(2)}, u32[]{:S(2)}) %collective-permute-start) | collective-permute-done | bytes 32800 | tf_op jit(solution)/shard_map/while/body/eval_jaxpr/ppermute | solution.py:14
  47.9 0.1 bitcast_add_fusion.2
  48.3 1.7 broadcast_multiply_fusion
  50.1 12.4 %while.42 = (s32[]{:T(128)}, bf16[2,128,32,128]{3,2,1,0:T(8,128)(2,1)}, s32[2]{0:T(128)S(1)}, bf16[1,8,32,2,128]{4,2,1,3,0:T(8,128)(2,1)S(1)}, bf16[128,1,32,8,3...) while((s32[]{:T(128)}, bf16[2,128,32,128]{3,2,1,0:T(8,128)(2,1)}, s32[2]{0:T(128)S(1)}, ...), condition=%wide.region_3.4_spmd, body=%wide.region_2.3_spmd.sunk | while | flops 268959744 | bytes 22085836 | solution.py:70
  50.1 0.6 dynamic_slice.40
  52.7 0.5 fusion.52
  53.1 1.1 copy-done.3
  54.3 0.7 copy_dynamic-update-slice_fusion.2
  55.0 1.3 copy-done.4
  56.3 0.6 dynamic_slice.40
  58.9 0.5 fusion.52
  59.3 1.1 copy-done.3
  60.4 0.7 copy_dynamic-update-slice_fusion.2
  61.2 1.3 copy-done.4
  62.5 3.6 %all-to-all-start = ((bf16[256,32,128]{2,1,0:T(8,128)(2,1)}), bf16[256,32,128]{2,1,0:T(8,128)(2,1)S(1)}, u32[]{:S(2)}, u32[]{:S(2)}) async-start(bf16[256,32,128]{2,1,0:T(8,128)(2,1)} %bitcast.132), calls=%async_computation | async-start | bytes 4194304 | tf_op jit(solution)/shard_map/all_to_all | solution.py:73
  66.2 26.5 %all-to-all-done = bf16[256,32,128]{2,1,0:T(8,128)(2,1)S(1)} async-done(((bf16[256,32,128]{2,1,0:T(8,128)(2,1)}), bf16[256,32,128]{2,1,0:T(8,128)(2,1)S(1)}, u32[]{:S(2)}, u32[]{:S(2)}) %all-to-all-start) | async-done | bytes 2097184 | tf_op jit(solution)/shard_map/all_to_all | solution.py:73
  92.7 1.3 copy-done.2
  94.0 2.2 copy.47
  96.3 67.1 %all-gather.2.cloned.1.call-done = bf16[512,32,256]{2,1,0:T(8,128)(2,1)} async-done(((bf16[128,32,256]{2,1,0:T(8,128)(2,1)}), bf16[512,32,256]{2,1,0:T(8,128)(2,1)}) %all-gather.2.cloned.1.call-update) | async-done | bytes 8388624 | tf_op jit(solution)/shard_map/all_gather | solution.py:82
  163.4 13.8 %copy.42 = bf16[512,32,256]{0,2,1:T(8,128)(2,1)} copy(bf16[512,32,256]{2,1,0:T(8,128)(2,1)} %all-gather.2.cloned.1.call-done) | data formatting | bytes 16777216 | tf_op jit(solution)/shard_map/all_gather | solution.py:82
  177.2 11.8 %while.43 = (s32[]{:T(128)}, f32[512,128]{1,0:T(8,128)S(1)}, bf16[1,8,32,256]{3,2,1,0:T(8,128)(2,1)S(1)}, bf16[512,1,32,8,32]{0,4,3,2,1:T(8,128)(2,1)}, bf16[32,...) while((s32[]{:T(128)}, f32[512,128]{1,0:T(8,128)S(1)}, ...), condition=%wide.region_5.6_spmd.clone, body=%wide.region_4.5_spmd.clone.sunk | while | flops 1612840960 | bytes 10028700 | solution.py:95
  177.2 5.9 %fusion.57 = f32[512,128]{1,0:T(8,128)S(1)} fusion(bf16[512,1,32,8,32]{0,4,3,2,1:T(8,128)(2,1)} %get-tuple-element.511, bf16[32,256,128]{2,1,0:T(8,128)(2,1)S(1)} %get-tuple-element.512, s32[]{:T(128)S(6)} %select_n.38, f32[512,128]{1,0:T(8,128)S(1)} %get-tuple-element.500, pred[]{:T(512)S(6)} %compare.4, ...), kind=kOutput, calls=%fused_computation.17.clone.1 | convolution fusion | flops 1612840960 | bytes 10028544 | tf_op jit(solution)/shard_map/while/body/eval_jaxpr/qln,lnp->qp/dot_general | solution.py:90
  183.1 5.9 %fusion.57 = f32[512,128]{1,0:T(8,128)S(1)} fusion(bf16[512,1,32,8,32]{0,4,3,2,1:T(8,128)(2,1)} %get-tuple-element.511, bf16[32,256,128]{2,1,0:T(8,128)(2,1)S(1)} %get-tuple-element.512, s32[]{:T(128)S(6)} %select_n.38, f32[512,128]{1,0:T(8,128)S(1)} %get-tuple-element.500, pred[]{:T(512)S(6)} %compare.4, ...), kind=kOutput, calls=%fused_computation.17.clone.1 | convolution fusion | flops 1612840960 | bytes 10028544 | tf_op jit(solution)/shard_map/while/body/eval_jaxpr/qln,lnp->qp/dot_general | solution.py:90
  189.0 0.7 copy-done
  189.7 32.0 %reduce-scatter.2.cloned.1.call-done = f32[64,128]{1,0:T(8,128)} async-done(((f32[512,128]{1,0:T(8,128)}), f32[64,128]{1,0:T(8,128)}) %reduce-scatter.2.cloned.1.call-update) | async-done | bytes 32784 | tf_op jit(solution)/shard_map/reduce_scatter | solution.py:94
  (66 shorter events, 1.2 us)
Async XLA Ops:
  6.5 156.8 %all-gather.2.cloned.1.call-start = ((), (), s32[]{:S(2)}) async-start(), calls=%async_computation.2 | async-start | bytes 10485760 | tf_op jit(solution)/shard_map/all_gather | solution.py:82
  10.8 1.6 copy-start.1
  12.4 3.1 %copy-start.7 = (s32[1,8]{1,0:T(1,128)S(1)}, s32[1,8]{1,0:T(1,128)}, u32[]{:S(2)}) copy-start(s32[1,8]{1,0:T(1,128)} %param.18) | copy-start | bytes 100
  12.4 3.3 %copy-start.8 = (s32[1,8]{1,0:T(1,128)S(1)}, s32[1,8]{1,0:T(1,128)}, u32[]{:S(2)}) copy-start(s32[1,8]{1,0:T(1,128)} %param.17) | copy-start | bytes 100
  12.4 3.5 %copy-start.5 = (bf16[32,256]{1,0:T(8,128)(2,1)S(1)}, bf16[32,256]{1,0:T(8,128)(2,1)}, u32[]{:S(2)}) copy-start(bf16[32,256]{1,0:T(8,128)(2,1)} %param.16) | copy-start | bytes 49156
  12.4 3.5 %copy-start.6 = (bf16[32,256]{1,0:T(8,128)(2,1)S(1)}, bf16[32,256]{1,0:T(8,128)(2,1)}, u32[]{:S(2)}) copy-start(bf16[32,256]{1,0:T(8,128)(2,1)} %param.15) | copy-start | bytes 49156
  12.4 3.5 %copy-start.9 = (s32[1,8]{1,0:T(1,128)S(1)}, s32[1,8]{1,0:T(1,128)}, u32[]{:S(2)}) copy-start(s32[1,8]{1,0:T(1,128)} %param.19) | copy-start | bytes 100
  16.1 5.0 %collective-permute-start = (bf16[2,32,256]{2,1,0:T(8,128)(2,1)S(1)}, bf16[2,32,256]{2,1,0:T(8,128)(2,1)S(1)}, u32[]{:S(2)}, u32[]{:S(2)}) collective-permute-start(bf16[2,32,256]{2,1,0:T(8,128)(2,1)S(1)} %get-tuple-element.449), channel_id=1, source_target_pairs={{7,0},{0,1},{1,2},{2,3},{3,4},{4,5},{5,6},{6,7},{15,8},{8,9},{9,10... | collective-permute-start | bytes 98312 | tf_op jit(solution)/shard_map/while/body/eval_jaxpr/ppermute | solution.py:14
  21.2 4.3 %collective-permute-start = (bf16[2,32,256]{2,1,0:T(8,128)(2,1)S(1)}, bf16[2,32,256]{2,1,0:T(8,128)(2,1)S(1)}, u32[]{:S(2)}, u32[]{:S(2)}) collective-permute-start(bf16[2,32,256]{2,1,0:T(8,128)(2,1)S(1)} %get-tuple-element.449), channel_id=1, source_target_pairs={{7,0},{0,1},{1,2},{2,3},{3,4},{4,5},{5,6},{6,7},{15,8},{8,9},{9,10... | collective-permute-start | bytes 98312 | tf_op jit(solution)/shard_map/while/body/eval_jaxpr/ppermute | solution.py:14
  25.7 4.3 %collective-permute-start = (bf16[2,32,256]{2,1,0:T(8,128)(2,1)S(1)}, bf16[2,32,256]{2,1,0:T(8,128)(2,1)S(1)}, u32[]{:S(2)}, u32[]{:S(2)}) collective-permute-start(bf16[2,32,256]{2,1,0:T(8,128)(2,1)S(1)} %get-tuple-element.449), channel_id=1, source_target_pairs={{7,0},{0,1},{1,2},{2,3},{3,4},{4,5},{5,6},{6,7},{15,8},{8,9},{9,10... | collective-permute-start | bytes 98312 | tf_op jit(solution)/shard_map/while/body/eval_jaxpr/ppermute | solution.py:14
  30.2 4.3 %collective-permute-start = (bf16[2,32,256]{2,1,0:T(8,128)(2,1)S(1)}, bf16[2,32,256]{2,1,0:T(8,128)(2,1)S(1)}, u32[]{:S(2)}, u32[]{:S(2)}) collective-permute-start(bf16[2,32,256]{2,1,0:T(8,128)(2,1)S(1)} %get-tuple-element.449), channel_id=1, source_target_pairs={{7,0},{0,1},{1,2},{2,3},{3,4},{4,5},{5,6},{6,7},{15,8},{8,9},{9,10... | collective-permute-start | bytes 98312 | tf_op jit(solution)/shard_map/while/body/eval_jaxpr/ppermute | solution.py:14
  34.7 4.3 %collective-permute-start = (bf16[2,32,256]{2,1,0:T(8,128)(2,1)S(1)}, bf16[2,32,256]{2,1,0:T(8,128)(2,1)S(1)}, u32[]{:S(2)}, u32[]{:S(2)}) collective-permute-start(bf16[2,32,256]{2,1,0:T(8,128)(2,1)S(1)} %get-tuple-element.449), channel_id=1, source_target_pairs={{7,0},{0,1},{1,2},{2,3},{3,4},{4,5},{5,6},{6,7},{15,8},{8,9},{9,10... | collective-permute-start | bytes 98312 | tf_op jit(solution)/shard_map/while/body/eval_jaxpr/ppermute | solution.py:14
  39.1 4.3 %collective-permute-start = (bf16[2,32,256]{2,1,0:T(8,128)(2,1)S(1)}, bf16[2,32,256]{2,1,0:T(8,128)(2,1)S(1)}, u32[]{:S(2)}, u32[]{:S(2)}) collective-permute-start(bf16[2,32,256]{2,1,0:T(8,128)(2,1)S(1)} %get-tuple-element.449), channel_id=1, source_target_pairs={{7,0},{0,1},{1,2},{2,3},{3,4},{4,5},{5,6},{6,7},{15,8},{8,9},{9,10... | collective-permute-start | bytes 98312 | tf_op jit(solution)/shard_map/while/body/eval_jaxpr/ppermute | solution.py:14
  43.6 4.3 %collective-permute-start = (bf16[2,32,256]{2,1,0:T(8,128)(2,1)S(1)}, bf16[2,32,256]{2,1,0:T(8,128)(2,1)S(1)}, u32[]{:S(2)}, u32[]{:S(2)}) collective-permute-start(bf16[2,32,256]{2,1,0:T(8,128)(2,1)S(1)} %get-tuple-element.449), channel_id=1, source_target_pairs={{7,0},{0,1},{1,2},{2,3},{3,4},{4,5},{5,6},{6,7},{15,8},{8,9},{9,10... | collective-permute-start | bytes 98312 | tf_op jit(solution)/shard_map/while/body/eval_jaxpr/ppermute | solution.py:14
  52.6 1.6 copy-start.3
  55.0 1.3 copy-start.4
  58.9 1.6 copy-start.3
  61.2 1.3 copy-start.4
  62.5 30.2 %all-to-all-start = ((bf16[256,32,128]{2,1,0:T(8,128)(2,1)}), bf16[256,32,128]{2,1,0:T(8,128)(2,1)S(1)}, u32[]{:S(2)}, u32[]{:S(2)}) async-start(bf16[256,32,128]{2,1,0:T(8,128)(2,1)} %bitcast.132), calls=%async_computation | async-start | bytes 4194304 | tf_op jit(solution)/shard_map/all_to_all | solution.py:73
  66.1 155.6 %reduce-scatter.2.cloned.1.call-start = ((), (), s32[]{:S(2)}) async-start(), calls=%async_computation.3 | async-start | bytes 294912 | tf_op jit(solution)/shard_map/reduce_scatter | solution.py:94
  92.7 1.3 copy-start.2
  189.0 0.7 copy-start
Sparse Core Ops, SparseCore 0:
  11.0 152.3 all-gather.1
  189.8 31.8 reduce-scatter.1
where the time goes:
time: 229 us
  waiting for transfers between devices  155 us (68%)
  local copies, waits for them, and re-layouts  31.3 us (14%)
  between operations  13.6 us (6%)
  matrix products  12.7 us (6%)
  other arithmetic  6.8 us (3%)
  starting transfers between devices  4.5 us (2%)
  loops' own time  4.39 us (2%)
    all_gather x1, waiting for transfers between devices, per_device(): all_tensor = lax.all_gather(tensor_eff, 'ri', axis=0, tiled=True)  67.1 us
    reduce_scatter x1, waiting for transfers between devices, per_device(): lax.psum_scatter(lax.fori_loop(0, piece_count, add_piece, jnp.zeros((pola...  32 us
    ppermute x7, waiting for transfers between devices, shifted(): return lax.ppermute(block, axis, route)  29.6 us
    all_to_all x1, waiting for transfers between devices, per_device(): lax.all_to_all(half_occ, 'ao', split_axis=0, concat_axis=1, tiled=True)  26.5 us
    all_gather x1, local copies, waits for them, and re-layouts, per_device(): all_tensor = lax.all_gather(tensor_eff, 'ri', axis=0, tiled=True)  13.8 us
    dot_general x2, matrix products, add_piece(): jnp.einsum('qln,lnp->qp', virt_part, occ_part, preferred_element_type=jnp...  11.8 us
    unnamed x17, local copies, waits for them, and re-layouts  6.7 us
    while x15, local copies, waits for them, and re-layouts  4.9 us
  transfers between devices with their start and end apart: 10, of which 10 were waited for; matrix products, arithmetic and copies ran while one was open for 5% of the time, Pallas kernels for 0%

commit v1 on v0

--- a/solution.py
+++ b/solution.py
@@ -70,7 +70,15 @@
     half_occ = lax.map(occ_piece, jnp.arange(piece_count, dtype=jnp.int32)).reshape(
         ao_total, own_width, own_rows
     )
-    half_occ_local = lax.all_to_all(half_occ, "ao", split_axis=0, concat_axis=1, tiled=True)
+
+    def _raise_sources_all(arr_in):
+        t_next = lax.axis_size("ao")
+        arr_next = jnp.split(arr_in, t_next, 0)
+        prior = jnp.stack(arr_next)
+        fresh = lax.all_to_all(prior, axis_name="ao", split_axis=0, concat_axis=0)
+        return jnp.concatenate(fresh, 1)
+
+    half_occ_local = _raise_sources_all(half_occ)
 
     def virt_piece(source_rows, piece_index):
         columns = lax.dynamic_slice_in_dim(virt_rows, piece_index * span_cols, span_cols, 3)

time: 229 us -> 229 us (level)
  waiting for transfers between devices: 155 us -> 145 us
  local copies, waits for them, and re-layouts: 31.3 us -> 41 us
    all_gather x1, waiting for transfers between devices: 67.1 us -> 57.3 us  [per_device(): all_tensor = lax.all_gather(tensor_eff, 'ri', axis=0, tiled=True)]
    unnamed x17 -> x26, local copies, waits for them, and re-layouts: 6.7 us -> 15.7 us
  transfers between devices with their start and end apart: 10 -> 10, of which waited for: 10 -> 10; matrix products, arithmetic and copies ran while one was open for 5% -> 10% of each run, Pallas kernels for 0% -> 0%
where the time goes in v1:
time: 229 us
  waiting for transfers between devices  145 us (63%)
  local copies, waits for them, and re-layouts  41 us (18%)
  between operations  13.6 us (6%)
  matrix products  12.7 us (6%)
  other arithmetic  6.8 us (3%)
  starting transfers between devices  4.5 us (2%)
  loops' own time  4.39 us (2%)
    all_gather x1, waiting for transfers between devices, per_device(): all_tensor = lax.all_gather(tensor_eff, 'ri', axis=0, tiled=True)  57.3 us
    reduce_scatter x1, waiting for transfers between devices, per_device(): lax.psum_scatter(lax.fori_loop(0, piece_count, add_piece, jnp.zeros((pola...  32 us
    ppermute x7, waiting for transfers between devices, shifted(): return lax.ppermute(block, axis, route)  29.6 us
    all_to_all x1, waiting for transfers between devices, _raise_sources_all(): fresh = lax.all_to_all(prior, axis_name='ao', split_axis=0, concat_axis=0)  26.5 us
    unnamed x26, local copies, waits for them, and re-layouts  15.7 us
    all_gather x1, local copies, waits for them, and re-layouts, per_device(): all_tensor = lax.all_gather(tensor_eff, 'ri', axis=0, tiled=True)  13.8 us
    dot_general x2, matrix products, add_piece(): jnp.einsum('qln,lnp->qp', virt_part, occ_part, preferred_element_type=jnp...  11.8 us
    while x15, local copies, waits for them, and re-layouts  4.92 us
  transfers between devices with their start and end apart: 10, of which 10 were waited for; matrix products, arithmetic and copies ran while one was open for 10% of the time, Pallas kernels for 0%

profile of v1, /device:TPU:0, one launch (start us, length us, event | category | flops | bytes accessed | tf_op | source)
XLA Modules:
  0.0 228.5 jit_solution(676546712682296193)
XLA Ops:
  6.5 0.7 convert_element_type.41
  7.7 3.1 %broadcast_multiply_fusion.1 = bf16[128,32,256]{2,1,0:T(8,128)(2,1)} fusion(bf16[128,32,256]{2,1,0:T(8,128)(2,1)} %param.13, bf16[128,256]{1,0:T(8,128)(2,1)S(1)} %copy.48), kind=kLoop, calls=%fused_computation.23 | loop fusion | flops 1048576 | bytes 4259840 | tf_op jit(solution)/shard_map/mul | solution.py:39
  10.9 1.6 copy-done.1
  12.5 3.1 %copy.50 = bf16[128,32,256]{0,2,1:T(8,128)(2,1)} copy(bf16[128,32,256]{2,1,0:T(8,128)(2,1)S(1)} %copy-done.1) | data formatting | bytes 4194304 | tf_op args[0]
  16.1 32.0 %while.41 = (s32[]{:T(128)}, bf16[2,32,256]{2,1,0:T(8,128)(2,1)S(1)}, f32[2,1,8,32,256]{4,3,2,1,0:T(8,128)S(1)}, s32[]{:T(128)}, s32[1,8]{1,0:T(1,128)S(1)}, /*index=5*/s32[]{:T(128)}, s32[]{:T(128)}, s32[]{:T(128)}, s32[]{:T(128)}) while((s32[]{:T(128)}, bf16[2,32,256]{2,1,0:T(8,128)(2,1)S(1)}, f32[2,1,8,32,256]{4,3,2,1,0:T(8,128)S(1)}, ...), condition=%wide.region_1.2_spmd, body=%wide.region_0.1_spmd.sunk | while | flops 278559 | bytes 1409390 | solution.py:54
  16.1 0.5 collective-permute-start
  16.6 4.5 %collective-permute-done = bf16[2,32,256]{2,1,0:T(8,128)(2,1)S(1)} collective-permute-done((bf16[2,32,256]{2,1,0:T(8,128)(2,1)S(1)}, bf16[2,32,256]{2,1,0:T(8,128)(2,1)S(1)}, u32[]{:S(2)}, u32[]{:S(2)}) %collective-permute-start) | collective-permute-done | bytes 32800 | tf_op jit(solution)/shard_map/while/body/eval_jaxpr/ppermute | solution.py:14
  21.1 0.1 bitcast_add_fusion.2
  21.4 4.2 %collective-permute-done = bf16[2,32,256]{2,1,0:T(8,128)(2,1)S(1)} collective-permute-done((bf16[2,32,256]{2,1,0:T(8,128)(2,1)S(1)}, bf16[2,32,256]{2,1,0:T(8,128)(2,1)S(1)}, u32[]{:S(2)}, u32[]{:S(2)}) %collective-permute-start) | collective-permute-done | bytes 32800 | tf_op jit(solution)/shard_map/while/body/eval_jaxpr/ppermute | solution.py:14
  25.6 0.1 bitcast_add_fusion.2
  25.8 4.2 %collective-permute-done = bf16[2,32,256]{2,1,0:T(8,128)(2,1)S(1)} collective-permute-done((bf16[2,32,256]{2,1,0:T(8,128)(2,1)S(1)}, bf16[2,32,256]{2,1,0:T(8,128)(2,1)S(1)}, u32[]{:S(2)}, u32[]{:S(2)}) %collective-permute-start) | collective-permute-done | bytes 32800 | tf_op jit(solution)/shard_map/while/body/eval_jaxpr/ppermute | solution.py:14
  30.0 0.1 bitcast_add_fusion.2
  30.3 4.2 %collective-permute-done = bf16[2,32,256]{2,1,0:T(8,128)(2,1)S(1)} collective-permute-done((bf16[2,32,256]{2,1,0:T(8,128)(2,1)S(1)}, bf16[2,32,256]{2,1,0:T(8,128)(2,1)S(1)}, u32[]{:S(2)}, u32[]{:S(2)}) %collective-permute-start) | collective-permute-done | bytes 32800 | tf_op jit(solution)/shard_map/while/body/eval_jaxpr/ppermute | solution.py:14
  34.5 0.1 bitcast_add_fusion.2
  34.8 4.2 %collective-permute-done = bf16[2,32,256]{2,1,0:T(8,128)(2,1)S(1)} collective-permute-done((bf16[2,32,256]{2,1,0:T(8,128)(2,1)S(1)}, bf16[2,32,256]{2,1,0:T(8,128)(2,1)S(1)}, u32[]{:S(2)}, u32[]{:S(2)}) %collective-permute-start) | collective-permute-done | bytes 32800 | tf_op jit(solution)/shard_map/while/body/eval_jaxpr/ppermute | solution.py:14
  39.2 4.2 %collective-permute-done = bf16[2,32,256]{2,1,0:T(8,128)(2,1)S(1)} collective-permute-done((bf16[2,32,256]{2,1,0:T(8,128)(2,1)S(1)}, bf16[2,32,256]{2,1,0:T(8,128)(2,1)S(1)}, u32[]{:S(2)}, u32[]{:S(2)}) %collective-permute-start) | collective-permute-done | bytes 32800 | tf_op jit(solution)/shard_map/while/body/eval_jaxpr/ppermute | solution.py:14
  43.7 4.2 %collective-permute-done = bf16[2,32,256]{2,1,0:T(8,128)(2,1)S(1)} collective-permute-done((bf16[2,32,256]{2,1,0:T(8,128)(2,1)S(1)}, bf16[2,32,256]{2,1,0:T(8,128)(2,1)S(1)}, u32[]{:S(2)}, u32[]{:S(2)}) %collective-permute-start) | collective-permute-done | bytes 32800 | tf_op jit(solution)/shard_map/while/body/eval_jaxpr/ppermute | solution.py:14
  48.4 1.7 broadcast_multiply_fusion
  50.1 12.4 %while.42 = (s32[]{:T(128)}, bf16[2,128,32,128]{3,2,1,0:T(8,128)(2,1)}, s32[2]{0:T(128)S(1)}, bf16[1,8,32,2,128]{4,2,1,3,0:T(8,128)(2,1)S(1)}, bf16[128,1,32,8,3...) while((s32[]{:T(128)}, bf16[2,128,32,128]{3,2,1,0:T(8,128)(2,1)}, s32[2]{0:T(128)S(1)}, ...), condition=%wide.region_3.4_spmd, body=%wide.region_2.3_spmd.sunk | while | flops 268959744 | bytes 22085836 | solution.py:70
  50.1 0.6 dynamic_slice.40
  52.7 0.5 fusion.60
  53.1 1.1 copy-done.3
  54.3 0.7 copy_dynamic-update-slice_fusion.2
  55.0 1.3 copy-done.4
  56.4 0.6 dynamic_slice.40
  58.9 0.5 fusion.60
  59.4 1.1 copy-done.3
  60.5 0.7 copy_dynamic-update-slice_fusion.2
  61.2 1.3 copy-done.4
  62.6 1.8 fusion.44
  64.4 1.7 fusion.43
  66.1 1.7 fusion.42
  67.8 1.7 fusion.41
  69.4 0.7 fusion.40
  70.2 0.7 fusion.39
  70.9 0.7 fusion.38
  71.6 0.7 fusion.37
  72.3 3.6 %all-to-all-start = ((bf16[8,32,32,128]{3,2,1,0:T(8,128)(2,1)}), bf16[8,32,32,128]{3,2,1,0:T(8,128)(2,1)S(1)}, u32[]{:S(2)}, u32[]{:S(2)}) async-start(bf16[8,32,32,128]{3,2,1,0:T(8,128)(2,1)} %fusion.37), calls=%async_computation | async-start | bytes 4194304 | tf_op jit(solution)/shard_map/all_to_all | solution.py:78
  76.0 26.5 %all-to-all-done = bf16[8,32,32,128]{3,2,1,0:T(8,128)(2,1)S(1)} async-done(((bf16[8,32,32,128]{3,2,1,0:T(8,128)(2,1)}), bf16[8,32,32,128]{3,2,1,0:T(8,128)(2,1)S(1)}, u32[]{:S(2)}, u32[]{:S(2)}) %all-to-all-start) | async-done | bytes 2097184 | tf_op jit(solution)/shard_map/all_to_all | solution.py:78
  102.5 1.3 copy-done.2
  103.8 2.2 copy.54
  106.0 57.3 %all-gather.2.cloned.1.call-done = bf16[512,32,256]{2,1,0:T(8,128)(2,1)} async-done(((bf16[128,32,256]{2,1,0:T(8,128)(2,1)}), bf16[512,32,256]{2,1,0:T(8,128)(2,1)}) %all-gather.2.cloned.1.call-update) | async-done | bytes 8388624 | tf_op jit(solution)/shard_map/all_gather | solution.py:90
  163.4 13.8 %copy.49 = bf16[512,32,256]{0,2,1:T(8,128)(2,1)} copy(bf16[512,32,256]{2,1,0:T(8,128)(2,1)} %all-gather.2.cloned.1.call-done) | data formatting | bytes 16777216 | tf_op jit(solution)/shard_map/all_gather | solution.py:90
  177.2 11.8 %while.43 = (s32[]{:T(128)}, f32[512,128]{1,0:T(8,128)S(1)}, bf16[1,8,32,256]{3,2,1,0:T(8,128)(2,1)S(1)}, bf16[512,1,32,8,32]{0,4,3,2,1:T(8,128)(2,1)}, bf16[32,...) while((s32[]{:T(128)}, f32[512,128]{1,0:T(8,128)S(1)}, ...), condition=%wide.region_5.6_spmd.clone, body=%wide.region_4.5_spmd.clone.sunk | while | flops 1612840960 | bytes 10028700 | solution.py:103
  177.2 5.9 %fusion.65 = f32[512,128]{1,0:T(8,128)S(1)} fusion(bf16[512,1,32,8,32]{0,4,3,2,1:T(8,128)(2,1)} %get-tuple-element.511, bf16[32,256,128]{2,1,0:T(8,128)(2,1)S(1)} %get-tuple-element.512, s32[]{:T(128)S(6)} %select_n.38, f32[512,128]{1,0:T(8,128)S(1)} %get-tuple-element.500, pred[]{:T(512)S(6)} %compare.4, ...), kind=kOutput, calls=%fused_computation.17.clone.1 | convolution fusion | flops 1612840960 | bytes 10028544 | tf_op jit(solution)/shard_map/while/body/eval_jaxpr/qln,lnp->qp/dot_general | solution.py:98
  183.1 5.9 %fusion.65 = f32[512,128]{1,0:T(8,128)S(1)} fusion(bf16[512,1,32,8,32]{0,4,3,2,1:T(8,128)(2,1)} %get-tuple-element.511, bf16[32,256,128]{2,1,0:T(8,128)(2,1)S(1)} %get-tuple-element.512, s32[]{:T(128)S(6)} %select_n.38, f32[512,128]{1,0:T(8,128)S(1)} %get-tuple-element.500, pred[]{:T(512)S(6)} %compare.4, ...), kind=kOutput, calls=%fused_computation.17.clone.1 | convolution fusion | flops 1612840960 | bytes 10028544 | tf_op jit(solution)/shard_map/while/body/eval_jaxpr/qln,lnp->qp/dot_general | solution.py:98
  189.0 0.7 copy-done
  189.7 32.0 %reduce-scatter.2.cloned.1.call-done = f32[64,128]{1,0:T(8,128)} async-done(((f32[512,128]{1,0:T(8,128)}), f32[64,128]{1,0:T(8,128)}) %reduce-scatter.2.cloned.1.call-update) | async-done | bytes 32784 | tf_op jit(solution)/shard_map/reduce_scatter | solution.py:102
  (76 shorter events, 2.2 us)
Async XLA Ops:
  6.5 156.8 %all-gather.2.cloned.1.call-start = ((), (), s32[]{:S(2)}) async-start(), calls=%async_computation.2 | async-start | bytes 10485760 | tf_op jit(solution)/shard_map/all_gather | solution.py:90
  10.8 1.6 copy-start.1
  12.4 3.1 %copy-start.8 = (s32[1,8]{1,0:T(1,128)S(1)}, s32[1,8]{1,0:T(1,128)}, u32[]{:S(2)}) copy-start(s32[1,8]{1,0:T(1,128)} %param.18) | copy-start | bytes 100
  12.4 3.3 %copy-start.9 = (s32[1,8]{1,0:T(1,128)S(1)}, s32[1,8]{1,0:T(1,128)}, u32[]{:S(2)}) copy-start(s32[1,8]{1,0:T(1,128)} %param.17) | copy-start | bytes 100
  12.4 3.5 %copy-start.6 = (bf16[32,256]{1,0:T(8,128)(2,1)S(1)}, bf16[32,256]{1,0:T(8,128)(2,1)}, u32[]{:S(2)}) copy-start(bf16[32,256]{1,0:T(8,128)(2,1)} %param.16) | copy-start | bytes 49156
  12.4 3.5 %copy-start.7 = (bf16[32,256]{1,0:T(8,128)(2,1)S(1)}, bf16[32,256]{1,0:T(8,128)(2,1)}, u32[]{:S(2)}) copy-start(bf16[32,256]{1,0:T(8,128)(2,1)} %param.15) | copy-start | bytes 49156
  12.4 3.5 %copy-start.10 = (s32[1,8]{1,0:T(1,128)S(1)}, s32[1,8]{1,0:T(1,128)}, u32[]{:S(2)}) copy-start(s32[1,8]{1,0:T(1,128)} %param.19) | copy-start | bytes 100
  16.1 5.0 %collective-permute-start = (bf16[2,32,256]{2,1,0:T(8,128)(2,1)S(1)}, bf16[2,32,256]{2,1,0:T(8,128)(2,1)S(1)}, u32[]{:S(2)}, u32[]{:S(2)}) collective-permute-start(bf16[2,32,256]{2,1,0:T(8,128)(2,1)S(1)} %get-tuple-element.449), channel_id=1, source_target_pairs={{7,0},{0,1},{1,2},{2,3},{3,4},{4,5},{5,6},{6,7},{15,8},{8,9},{9,10... | collective-permute-start | bytes 98312 | tf_op jit(solution)/shard_map/while/body/eval_jaxpr/ppermute | solution.py:14
  21.3 4.3 %collective-permute-start = (bf16[2,32,256]{2,1,0:T(8,128)(2,1)S(1)}, bf16[2,32,256]{2,1,0:T(8,128)(2,1)S(1)}, u32[]{:S(2)}, u32[]{:S(2)}) collective-permute-start(bf16[2,32,256]{2,1,0:T(8,128)(2,1)S(1)} %get-tuple-element.449), channel_id=1, source_target_pairs={{7,0},{0,1},{1,2},{2,3},{3,4},{4,5},{5,6},{6,7},{15,8},{8,9},{9,10... | collective-permute-start | bytes 98312 | tf_op jit(solution)/shard_map/while/body/eval_jaxpr/ppermute | solution.py:14
  25.7 4.3 %collective-permute-start = (bf16[2,32,256]{2,1,0:T(8,128)(2,1)S(1)}, bf16[2,32,256]{2,1,0:T(8,128)(2,1)S(1)}, u32[]{:S(2)}, u32[]{:S(2)}) collective-permute-start(bf16[2,32,256]{2,1,0:T(8,128)(2,1)S(1)} %get-tuple-element.449), channel_id=1, source_target_pairs={{7,0},{0,1},{1,2},{2,3},{3,4},{4,5},{5,6},{6,7},{15,8},{8,9},{9,10... | collective-permute-start | bytes 98312 | tf_op jit(solution)/shard_map/while/body/eval_jaxpr/ppermute | solution.py:14
  30.2 4.3 %collective-permute-start = (bf16[2,32,256]{2,1,0:T(8,128)(2,1)S(1)}, bf16[2,32,256]{2,1,0:T(8,128)(2,1)S(1)}, u32[]{:S(2)}, u32[]{:S(2)}) collective-permute-start(bf16[2,32,256]{2,1,0:T(8,128)(2,1)S(1)} %get-tuple-element.449), channel_id=1, source_target_pairs={{7,0},{0,1},{1,2},{2,3},{3,4},{4,5},{5,6},{6,7},{15,8},{8,9},{9,10... | collective-permute-start | bytes 98312 | tf_op jit(solution)/shard_map/while/body/eval_jaxpr/ppermute | solution.py:14
  34.7 4.3 %collective-permute-start = (bf16[2,32,256]{2,1,0:T(8,128)(2,1)S(1)}, bf16[2,32,256]{2,1,0:T(8,128)(2,1)S(1)}, u32[]{:S(2)}, u32[]{:S(2)}) collective-permute-start(bf16[2,32,256]{2,1,0:T(8,128)(2,1)S(1)} %get-tuple-element.449), channel_id=1, source_target_pairs={{7,0},{0,1},{1,2},{2,3},{3,4},{4,5},{5,6},{6,7},{15,8},{8,9},{9,10... | collective-permute-start | bytes 98312 | tf_op jit(solution)/shard_map/while/body/eval_jaxpr/ppermute | solution.py:14
  39.1 4.3 %collective-permute-start = (bf16[2,32,256]{2,1,0:T(8,128)(2,1)S(1)}, bf16[2,32,256]{2,1,0:T(8,128)(2,1)S(1)}, u32[]{:S(2)}, u32[]{:S(2)}) collective-permute-start(bf16[2,32,256]{2,1,0:T(8,128)(2,1)S(1)} %get-tuple-element.449), channel_id=1, source_target_pairs={{7,0},{0,1},{1,2},{2,3},{3,4},{4,5},{5,6},{6,7},{15,8},{8,9},{9,10... | collective-permute-start | bytes 98312 | tf_op jit(solution)/shard_map/while/body/eval_jaxpr/ppermute | solution.py:14
  43.6 4.3 %collective-permute-start = (bf16[2,32,256]{2,1,0:T(8,128)(2,1)S(1)}, bf16[2,32,256]{2,1,0:T(8,128)(2,1)S(1)}, u32[]{:S(2)}, u32[]{:S(2)}) collective-permute-start(bf16[2,32,256]{2,1,0:T(8,128)(2,1)S(1)} %get-tuple-element.449), channel_id=1, source_target_pairs={{7,0},{0,1},{1,2},{2,3},{3,4},{4,5},{5,6},{6,7},{15,8},{8,9},{9,10... | collective-permute-start | bytes 98312 | tf_op jit(solution)/shard_map/while/body/eval_jaxpr/ppermute | solution.py:14
  52.7 1.6 copy-start.3
  55.0 1.3 copy-start.4
  58.9 1.6 copy-start.3
  61.2 1.3 copy-start.4
  62.6 6.9 %copy-start.5 = (bf16[2,128,32,128]{3,2,1,0:T(8,128)(2,1)S(1)}, bf16[2,128,32,128]{3,2,1,0:T(8,128)(2,1)}, u32[]{:S(2)}) copy-start(bf16[2,128,32,128]{3,2,1,0:T(8,128)(2,1)} %get-tuple-element.260) | copy-start | bytes 6291460
  72.3 30.2 %all-to-all-start = ((bf16[8,32,32,128]{3,2,1,0:T(8,128)(2,1)}), bf16[8,32,32,128]{3,2,1,0:T(8,128)(2,1)S(1)}, u32[]{:S(2)}, u32[]{:S(2)}) async-start(bf16[8,32,32,128]{3,2,1,0:T(8,128)(2,1)} %fusion.37), calls=%async_computation | async-start | bytes 4194304 | tf_op jit(solution)/shard_map/all_to_all | solution.py:78
  75.9 145.8 %reduce-scatter.2.cloned.1.call-start = ((), (), s32[]{:S(2)}) async-start(), calls=%async_computation.3 | async-start | bytes 294912 | tf_op jit(solution)/shard_map/reduce_scatter | solution.py:102
  102.5 1.3 copy-start.2
  189.0 0.7 copy-start
Sparse Core Ops, SparseCore 0:
  11.0 152.3 all-gather.1
  189.8 31.8 reduce-scatter.1
